TPU v7x, 32 devices: a whole 2x2x4 slice. The times are simulated.
32 devices in a mesh: section: 2 (over core), fsdp: 2 (over y), expert: 8 (over z, x).
Axes of the slice: x: 2, y: 2, z: 4, core: 2. Of those that a mesh axis runs over, the one named last changes fastest.
Arguments:
- tokens: bfloat16 [2048, 2048], P(('fsdp', 'expert')), may hold values from -40 to 40
- norm_gain: float32 [2, 2048], P('section'), may hold values from 0.5 to 1.5
- router: bfloat16 [2, 2048, 32], P('section'), may hold values from -0.3125 to 0.3125
- w_gate: bfloat16 [2, 32, 2048, 768], P('section', 'expert', 'fsdp'), may hold values from -0.125 to 0.125
- w_up: bfloat16 [2, 32, 2048, 768], P('section', 'expert', 'fsdp'), may hold values from -0.125 to 0.125
- w_down: bfloat16 [2, 32, 768, 2048], P('section', 'expert', None, 'fsdp'), may hold values from -0.21875 to 0.21875
- routes: int32 [2, 2048, 6], P('section', ('fsdp', 'expert')), may hold values from 0 to 31, all different within a row; in each aligned block of 64 rows (0 to 63, 64 to 127, ..., all dimensions but the last counted through in order) at most 14 rows name the same one
Outputs:
- final_out: bfloat16 [2048, 2048], P(('fsdp', 'expert'), 'section')
- layer_stats: float32 [2], P('section')
Inputs may be any that keep to these rules, and one draw needn't show every extreme that they name: `routes`: each row names 6 different experts; in every aligned block of 64 rows of one layer no expert is named by more than 14 rows, a bound that some block reaches.
All inputs are finite; a program needn't handle non-finite values.
Results may differ from a plain program's by a relative error of at most 0.0065.
Values may be sent and summed in bfloat16 or wider, within the bound.
No kernel may reach another device: no remote copies, remote signals or barrier semaphores. Data moves between devices by JAX's collectives and lax.ppermute only.
A program may use at most 192 MiB of HBM per device.

v0:
```python
import jax
import jax.numpy as jnp
from jax import lax
from jax.sharding import PartitionSpec as P

TOP = 6
BLOCK = 64
epsilon = 1e-06


def other_section(value):
    return lax.ppermute(value, "section", [(0, 1), (1, 0)])


def rms_scaled(hidden_rows, gain_row):
    values = hidden_rows.astype(jnp.float32)
    scale = lax.rsqrt(jnp.mean(values * values, axis=-1, keepdims=True) + epsilon)
    return (values * scale * gain_row).astype(jnp.bfloat16)


def gate_weights(normed, router_weight, route_rows):
    logits = jnp.dot(normed, router_weight, preferred_element_type=jnp.float32)
    scores = jax.nn.sigmoid(logits)
    expert_ids = jnp.arange(router_weight.shape[1], dtype=jnp.int32)
    chosen_mask = (route_rows[:, :, None] == expert_ids[None, None, :]).astype(jnp.float32)
    chosen = jnp.sum(scores[:, None, :] * chosen_mask, axis=2)
    return chosen / jnp.sum(chosen, axis=1, keepdims=True)


def slot_positions(route_rows, experts_count, capacity):
    flat_routes = route_rows.reshape(-1)
    onehot = (flat_routes[:, None] == jnp.arange(experts_count, dtype=jnp.int32)[None, :]).astype(
        jnp.int32
    )
    before = jnp.cumsum(onehot, axis=0) - onehot
    slot_index = jnp.sum(before * onehot, axis=1)
    return (flat_routes * capacity + slot_index).reshape(route_rows.shape)


def expert_layer(entering, route_rows, gain_row, router_weight, weights, capacity):
    gate_w, up_w, down_w = weights
    width = entering.shape[1]
    experts_count = router_weight.shape[1]
    local_experts, chunk, hidden_units = gate_w.shape
    fsdp_count = lax.axis_size("fsdp")
    expert_devices = lax.axis_size("expert")
    peers = fsdp_count * expert_devices
    normed = rms_scaled(entering, gain_row)
    mix_weights = gate_weights(normed, router_weight, route_rows)
    positions = slot_positions(route_rows, experts_count, capacity)
    slot_ids = jnp.arange(experts_count * capacity, dtype=jnp.int32)
    placing = jnp.any(positions[None, :, :] == slot_ids[:, None, None], axis=2).astype(jnp.bfloat16)
    buffer = jnp.dot(placing, normed, preferred_element_type=jnp.float32).astype(jnp.bfloat16)
    outgoing = (
        buffer.reshape(expert_devices, local_experts * capacity, fsdp_count, chunk)
        .transpose(2, 0, 1, 3)
        .reshape(peers, local_experts * capacity, chunk)
    )
    arrived = lax.all_to_all(outgoing, ("fsdp", "expert"), 0, 0, tiled=True)
    arrived = arrived.reshape(peers, local_experts, capacity, chunk)
    gate_part = jnp.einsum("sjcd,jdh->sjch", arrived, gate_w, preferred_element_type=jnp.float32)
    up_part = jnp.einsum("sjcd,jdh->sjch", arrived, up_w, preferred_element_type=jnp.float32)
    both = jnp.concatenate([gate_part, up_part], axis=-1)
    summed = lax.psum_scatter(both, "fsdp", scatter_dimension=0, tiled=True)
    gate_sum = summed[..., :hidden_units]
    up_sum = summed[..., hidden_units:]
    inner_act = (jax.nn.silu(gate_sum) * up_sum).astype(jnp.bfloat16)
    inner_all = lax.all_gather(inner_act, "fsdp", axis=0, tiled=True)
    produced = jnp.einsum(
        "sjch,jhd->sjcd", inner_all, down_w, preferred_element_type=jnp.float32
    ).astype(jnp.bfloat16)
    returned = lax.all_to_all(
        produced.reshape(peers, local_experts * capacity, chunk),
        ("fsdp", "expert"),
        0,
        0,
        tiled=True,
    )
    flat_out = (
        returned.reshape(fsdp_count, expert_devices, local_experts * capacity, chunk)
        .transpose(1, 2, 0, 3)
        .reshape(experts_count * capacity, width)
    )
    picked = jnp.take(flat_out, positions, axis=0)
    branch_sum = jnp.sum(mix_weights[:, :, None] * picked.astype(jnp.float32), axis=1)
    return (entering.astype(jnp.float32) + branch_sum).astype(jnp.bfloat16)


def body(tokens, norm_gain, router, w_gate, w_up, w_down, routes):
    section_index = lax.axis_index("section")
    sections = lax.axis_size("section")
    token_rows, width = tokens.shape
    piece = token_rows // sections
    experts_count = router.shape[2]
    block_capacity = (7 * BLOCK * TOP + 6 * experts_count - 1) // (6 * experts_count)
    capacity = block_capacity * (piece // BLOCK)
    own_weights = (w_gate[0], w_up[0], w_down[0])
    other_weights = tuple((other_section(w) for w in own_weights))
    own_small = (norm_gain[0], router[0], routes[0])
    other_small = tuple((other_section(v) for v in own_small))
    hidden = lax.dynamic_slice_in_dim(tokens, section_index * piece, piece, 0)
    squares = []
    for layer in range(sections):
        mine = section_index == layer
        gain_row, router_weight, route_all = [
            jnp.where(mine, a, b) for a, b in zip(own_small, other_small)
        ]
        weights = tuple((jnp.where(mine, a, b) for a, b in zip(own_weights, other_weights)))
        route_rows = lax.dynamic_slice_in_dim(route_all, section_index * piece, piece, 0)
        hidden = expert_layer(hidden, route_rows, gain_row, router_weight, weights, capacity)
        values = hidden.astype(jnp.float32)
        squares.append(jnp.sum(values * values))
    totals = lax.psum(jnp.stack(squares), ("section", "fsdp", "expert"))
    token_total = token_rows * lax.axis_size("fsdp") * lax.axis_size("expert")
    stats = jnp.sqrt(totals / (token_total * width))
    layer_stats = lax.dynamic_slice_in_dim(stats, section_index, 1, 0)
    half_width = width // 2
    keep = lax.dynamic_slice_in_dim(hidden, section_index * half_width, half_width, 1)
    send = lax.dynamic_slice_in_dim(hidden, (1 - section_index) * half_width, half_width, 1)
    arrived = other_section(send)
    final_out = jnp.where(
        section_index == 0,
        jnp.concatenate([keep, arrived], axis=0),
        jnp.concatenate([arrived, keep], axis=0),
    )
    return (final_out, layer_stats)


def solution(mesh):
    in_specs = (
        P(("fsdp", "expert"), None),
        P("section", None),
        P("section", None, None),
        P("section", "expert", "fsdp", None),
        P("section", "expert", "fsdp", None),
        P("section", "expert", None, "fsdp"),
        P("section", ("fsdp", "expert"), None),
    )
    out_specs = (P(("fsdp", "expert"), "section"), P("section"))
    return jax.shard_map(body, mesh=mesh, in_specs=in_specs, out_specs=out_specs, check_vma=False)
```

profile of v0, /device:TPU:0, one launch (start us, length us, event | category | flops | bytes accessed | tf_op | source)
XLA Modules:
  0.0 542.5 jit_solution(15079160899732492798)
XLA Ops:
  7.2 0.6 collective-permute-start.4
  7.8 0.7 copy.100
  8.5 0.5 collective-permute-start.1
  9.0 1.1 fusion.54
  10.1 7.8 %collective-permute-done = s32[128,6]{0,1:T(8,128)S(1)} collective-permute-done((s32[128,6]{0,1:T(8,128)S(1)}, s32[128,6]{0,1:T(8,128)S(1)}, u32[]{:S(2)}, u32[]{:S(2)}) %collective-permute-start) | collective-permute-done | bytes 3104 | tf_op jit(solution)/shard_map/ppermute | solution.py:12
  17.9 0.7 broadcast_select_fusion.3
  19.1 0.9 reduce-window.14
  19.9 0.2 slice_reduce_fusion.1
  20.5 0.2 fusion.50
  20.7 0.7 broadcast_select_fusion
  21.4 2.9 convolution_convert_fusion.1
  24.3 4.6 reshape.156
  28.9 0.5 copy.66
  29.5 52.1 %all_to_all.20 = bf16[16,56,1024]{2,1,0:T(8,128)(2,1)S(1)} all-to-all(bf16[16,56,1024]{2,1,0:T(8,128)(2,1)S(1)} %bitcast.172), channel_id=1, replica_groups=mesh['section'=2,'fsdp'=2,'expert'=8] {'fsdp','expert'}, dimensions={0} | all-to-all | bytes 3670016 | tf_op jit(solution)/shard_map/all_to_all | solution.py:59
  81.5 1.0 copy.67
  82.6 4.6 fusion.27
  87.1 4.6 fusion.30
  91.7 3.1 pad_maximum_fusion
  94.8 0.5 all-gather.3.cloned.1.call-start
  95.3 2.0 collective-permute-start.3
  97.3 66.4 %reduce-scatter.3.cloned.1.call-done = f32[8,4,14,1536]{3,0,2,1:T(8,128)} async-done(((f32[16,4,14,1536]{3,0,2,1:T(8,128)}), f32[8,4,14,1536]{3,0,2,1:T(8,128)}) %reduce-scatter.3.cloned.1.call-update) | async-done | bytes 2752528 | tf_op jit(solution)/shard_map/reduce_scatter | solution.py:64
  163.7 3.0 fusion.43
  166.8 25.1 %all-gather.3.cloned.1.call-done = bf16[16,4,14,768]{3,0,2,1:T(8,128)(2,1)} async-done(((bf16[8,4,14,768]{3,0,2,1:T(8,128)(2,1)}), bf16[16,4,14,768]{3,0,2,1:T(8,128)(2,1)}) %all-gather.3.cloned.1.call-update) | async-done | bytes 1376272 | tf_op jit(solution)/shard_map/all_gather | solution.py:68
  191.9 4.9 fusion.24
  196.8 2.3 copy.68
  199.1 5.7 %all-to-all-start.1 = ((bf16[16,56,1024]{2,1,0:T(8,128)(2,1)}), bf16[16,56,1024]{2,1,0:T(8,128)(2,1)S(1)}, u32[]{:S(2)}, u32[]{:S(2)}) async-start(bf16[16,56,1024]{2,1,0:T(8,128)(2,1)} %copy.68), calls=%async_computation.2 | async-start | bytes 3670016 | tf_op jit(solution)/shard_map/all_to_all | solution.py:72
  204.9 1.2 collective-permute-start.2
  206.8 0.9 reduce-window.16
  207.6 0.2 slice_reduce_fusion
  208.6 0.3 fusion.49
  209.0 39.2 %all-to-all-done.1 = bf16[16,56,1024]{2,1,0:T(8,128)(2,1)S(1)} async-done(((bf16[16,56,1024]{2,1,0:T(8,128)(2,1)}), bf16[16,56,1024]{2,1,0:T(8,128)(2,1)S(1)}, u32[]{:S(2)}, u32[]{:S(2)}) %all-to-all-start.1) | async-done | bytes 1835040 | tf_op jit(solution)/shard_map/all_to_all | solution.py:72
  248.2 1.9 copy.69
  250.1 0.5 copy.91
  250.6 2.5 gather_fusion
  253.1 1.6 reshape.192
  254.7 4.2 multiply_reduce_fusion.1
  258.9 0.8 fusion.52
  259.7 0.7 convolution_convert_fusion
  260.4 2.3 reshape.163
  262.7 2.0 copy.77
  264.7 49.3 %all_to_all.21 = bf16[16,56,1024]{2,1,0:T(8,128)(2,1)S(1)} all-to-all(bf16[16,56,1024]{2,1,0:T(8,128)(2,1)S(1)} %bitcast.174), channel_id=1, replica_groups=mesh['section'=2,'fsdp'=2,'expert'=8] {'fsdp','expert'}, dimensions={0} | all-to-all | bytes 3670016 | tf_op jit(solution)/shard_map/all_to_all | solution.py:59
  314.0 1.0 copy.78
  315.0 6.4 %fusion.36 = f32[16,4,14,768]{3,0,2,1:T(8,128)S(1)} fusion(bf16[16,4,14,1024]{3,0,2,1:T(8,128)(2,1)S(1)} %bitcast.178, bf16[4,1024,768]{2,1,0:T(8,128)(2,1)} %collective-permute-done.4, pred[]{:T(512)S(6)} %eq.124, bf16[1,4,1024,768]{3,2,1,0:T(8,128)(2,1)} %param.12), kind=kOutput, calls=%fused_computation.36 | convolution fusion | flops 1412431872 | bytes 17170432 | tf_op jit(solution)/shard_map/sjcd,jdh->sjch/dot_general | solution.py:61
  321.4 6.4 %fusion.39 = f32[16,4,14,768]{3,0,2,1:T(8,128)S(1)} fusion(bf16[16,4,14,1024]{3,0,2,1:T(8,128)(2,1)S(1)} %bitcast.179, bf16[4,1024,768]{2,1,0:T(8,128)(2,1)} %collective-permute-done.5, pred[]{:T(512)S(6)} %eq.124, bf16[1,4,1024,768]{3,2,1,0:T(8,128)(2,1)} %param.13), kind=kOutput, calls=%fused_computation.37 | convolution fusion | flops 1412431872 | bytes 17170432 | tf_op jit(solution)/shard_map/sjcd,jdh->sjch/dot_general | solution.py:62
  327.8 3.1 pad_maximum_fusion.1
  331.0 66.3 %reduce-scatter.5.cloned.1.call-done = f32[8,4,14,1536]{3,0,2,1:T(8,128)} async-done(((f32[16,4,14,1536]{3,0,2,1:T(8,128)}), f32[8,4,14,1536]{3,0,2,1:T(8,128)}) %reduce-scatter.5.cloned.1.call-update) | async-done | bytes 2752528 | tf_op jit(solution)/shard_map/reduce_scatter | solution.py:64
  397.3 3.0 fusion.42
  400.3 25.1 %all-gather.5.cloned.1.call-done = bf16[16,4,14,768]{3,0,2,1:T(8,128)(2,1)} async-done(((bf16[8,4,14,768]{3,0,2,1:T(8,128)(2,1)}), bf16[16,4,14,768]{3,0,2,1:T(8,128)(2,1)}) %all-gather.5.cloned.1.call-update) | async-done | bytes 1376272 | tf_op jit(solution)/shard_map/all_gather | solution.py:68
  425.5 6.7 %fusion.33 = bf16[4,1024,16,14]{1,2,3,0:T(8,128)(2,1)S(1)} fusion(bf16[16,4,14,768]{3,0,2,1:T(8,128)(2,1)} %all-gather.5.cloned.1.call-done, bf16[4,768,1024]{2,1,0:T(8,128)(2,1)} %collective-permute-done.3, pred[]{:T(512)S(6)} %eq.124, bf16[1,4,768,1024]{3,2,1,0:T(8,128)(2,1)} %param.14), kind=kOutput, calls=%fused_computation.35 | convolution fusion | flops 1413349376 | bytes 15794177 | tf_op jit(solution)/shard_map/sjch,jhd->sjcd/dot_general | solution.py:69
  432.2 2.3 copy.79
  434.4 6.0 %all-to-all-start.3 = ((bf16[16,56,1024]{2,1,0:T(8,128)(2,1)}), bf16[16,56,1024]{2,1,0:T(8,128)(2,1)S(1)}, u32[]{:S(2)}, u32[]{:S(2)}) async-start(bf16[16,56,1024]{2,1,0:T(8,128)(2,1)} %copy.79), calls=%async_computation.5 | async-start | bytes 3670016 | tf_op jit(solution)/shard_map/all_to_all | solution.py:72
  440.8 0.3 fusion.46
  441.3 40.0 %all-to-all-done.3 = bf16[16,56,1024]{2,1,0:T(8,128)(2,1)S(1)} async-done(((bf16[16,56,1024]{2,1,0:T(8,128)(2,1)}), bf16[16,56,1024]{2,1,0:T(8,128)(2,1)S(1)}, u32[]{:S(2)}, u32[]{:S(2)}) %all-to-all-start.3) | async-done | bytes 1835040 | tf_op jit(solution)/shard_map/all_to_all | solution.py:72
  481.3 1.9 copy.80
  483.2 0.5 copy.92
  483.7 2.5 gather_fusion.1
  486.2 1.6 reshape.196
  487.8 4.2 multiply_reduce_fusion
  492.0 0.7 multiply_reduce_fusion.2
  492.8 1.4 pad_maximum_fusion.2
  494.1 39.4 %psum.7 = f32[2]{0:T(128)S(1)} all-reduce(f32[2]{0:T(128)S(1)} %pad_maximum_fusion.2), channel_id=1, replica_groups=mesh['section'=2,'fsdp'=2,'expert'=8] {'section','fsdp','expert'}, use_global_device_ids=true, to_apply=%region_20.22 | all-reduce | flops 2 | bytes 16 | tf_op jit(solution)/shard_map/psum | solution.py:113
  533.7 0.6 dynamic_slice.23
  534.3 0.7 collective-permute-done.6
  535.0 0.8 maximum_select_fusion
  (71 shorter events, 3.1 us)
Async XLA Ops:
  7.2 156.6 %reduce-scatter.3.cloned.1.call-start = ((), (), s32[]{:S(2)}) async-start(), calls=%async_computation.6 | async-start | bytes 8257536 | tf_op jit(solution)/shard_map/reduce_scatter | solution.py:64
  7.2 75.3 %collective-permute-start.4 = (bf16[4,1024,768]{2,1,0:T(8,128)(2,1)}, bf16[4,1024,768]{2,1,0:T(8,128)(2,1)}, u32[]{:S(2)}, u32[]{:S(2)}) collective-permute-start(bf16[4,1024,768]{2,1,0:T(8,128)(2,1)} %bitcast.187), channel_id=1, source_target_pairs={{0,16},{16,0},{1,17},{17,1},{2,18},{18,2},{3,19},{19,3},{4,20},{20... | collective-permute-start | bytes 18874376 | tf_op jit(solution)/shard_map/ppermute | solution.py:12
  8.5 9.4 %collective-permute-start = (s32[128,6]{0,1:T(8,128)S(1)}, s32[128,6]{0,1:T(8,128)S(1)}, u32[]{:S(2)}, u32[]{:S(2)}) collective-permute-start(s32[128,6]{0,1:T(8,128)S(1)} %bitcast.186), channel_id=1, source_target_pairs={{0,16},{16,0},{1,17},{17,1},{2,18},{18,2},{3,19},{19,3},{4,20},{20... | collective-permute-start | bytes 9224 | tf_op jit(solution)/shard_map/ppermute | solution.py:12
  8.5 12.2 %collective-permute-start.1 = (f32[2048]{0:T(1024)}, f32[2048]{0:T(1024)S(1)}, u32[]{:S(2)}, u32[]{:S(2)}) collective-permute-start(f32[2048]{0:T(1024)} %bitcast.184), channel_id=1, source_target_pairs={{0,16},{16,0},{1,17},{17,1},{2,18},{18,2},{3,19},{19,3},{4,20},{20... | collective-permute-start | bytes 24584 | tf_op jit(solution)/shard_map/ppermute | solution.py:12
  9.0 78.2 %collective-permute-start.5 = (bf16[4,1024,768]{2,1,0:T(8,128)(2,1)}, bf16[4,1024,768]{2,1,0:T(8,128)(2,1)}, u32[]{:S(2)}, u32[]{:S(2)}) collective-permute-start(bf16[4,1024,768]{2,1,0:T(8,128)(2,1)} %bitcast.188), channel_id=1, source_target_pairs={{0,16},{16,0},{1,17},{17,1},{2,18},{18,2},{3,19},{19,3},{4,20},{20... | collective-permute-start | bytes 18874376 | tf_op jit(solution)/shard_map/ppermute | solution.py:12
  94.8 97.1 %all-gather.3.cloned.1.call-start = ((), (), s32[]{:S(2)}) async-start(), calls=%async_computation.7 | async-start | bytes 2064384 | tf_op jit(solution)/shard_map/all_gather | solution.py:68
  95.3 71.4 %collective-permute-start.3 = (bf16[4,768,1024]{2,1,0:T(8,128)(2,1)}, bf16[4,768,1024]{2,1,0:T(8,128)(2,1)}, u32[]{:S(2)}, u32[]{:S(2)}) collective-permute-start(bf16[4,768,1024]{2,1,0:T(8,128)(2,1)} %bitcast.189), channel_id=1, source_target_pairs={{0,16},{16,0},{1,17},{17,1},{2,18},{18,2},{3,19},{19,3},{4,20},{20... | collective-permute-start | bytes 18874376 | tf_op jit(solution)/shard_map/ppermute | solution.py:12
  199.1 5.8 %copy-start.4 = (bf16[1,2048,32]{1,2,0:T(8,128)(2,1)S(1)}, bf16[1,2048,32]{1,2,0:T(8,128)(2,1)}, u32[]{:S(2)}) copy-start(bf16[1,2048,32]{1,2,0:T(8,128)(2,1)} %param.11) | copy-start | bytes 393220
  199.1 9.5 %copy-start.2 = (bf16[128,2048]{1,0:T(8,128)(2,1)S(1)}, bf16[128,2048]{1,0:T(8,128)(2,1)}, u32[]{:S(2)}) copy-start(bf16[128,2048]{1,0:T(8,128)(2,1)} %param.9) | copy-start | bytes 1572868
  199.1 49.1 %all-to-all-start.1 = ((bf16[16,56,1024]{2,1,0:T(8,128)(2,1)}), bf16[16,56,1024]{2,1,0:T(8,128)(2,1)S(1)}, u32[]{:S(2)}, u32[]{:S(2)}) async-start(bf16[16,56,1024]{2,1,0:T(8,128)(2,1)} %copy.68), calls=%async_computation.2 | async-start | bytes 3670016 | tf_op jit(solution)/shard_map/all_to_all | solution.py:72
  204.8 192.5 %reduce-scatter.5.cloned.1.call-start = ((), (), s32[]{:S(2)}) async-start(), calls=%async_computation.8 | async-start | bytes 8257536 | tf_op jit(solution)/shard_map/reduce_scatter | solution.py:64
  204.9 3.7 collective-permute-start.2
  208.6 42.0 %copy-start.6 = (bf16[2048,32]{0,1:T(8,128)(2,1)}, bf16[2048,32]{0,1:T(8,128)(2,1)S(1)}, u32[]{:S(2)}) copy-start(bf16[2048,32]{0,1:T(8,128)(2,1)S(1)} %collective-permute-done.2) | copy-start | bytes 393220
  253.1 5.8 %copy-start.3 = (bf16[128,2048]{1,0:T(8,128)(2,1)S(1)}, bf16[128,2048]{1,0:T(8,128)(2,1)}, u32[]{:S(2)}) copy-start(bf16[128,2048]{1,0:T(8,128)(2,1)} %param.9) | copy-start | bytes 1572868
  259.7 181.1 %copy-start = (bf16[64,2048]{1,0:T(8,128)(2,1)}, bf16[64,2048]{1,0:T(8,128)(2,1)S(1)}, u32[]{:S(2)}) copy-start(bf16[64,2048]{1,0:T(8,128)(2,1)S(1)} %get-tuple-element.13) | copy-start | bytes 786436
  331.0 94.5 %all-gather.5.cloned.1.call-start = ((), (), s32[]{:S(2)}) async-start(), calls=%async_computation.9 | async-start | bytes 2064384 | tf_op jit(solution)/shard_map/all_gather | solution.py:68
  434.4 6.4 %copy-start.5 = (bf16[1,2048,32]{1,2,0:T(8,128)(2,1)S(1)}, bf16[1,2048,32]{1,2,0:T(8,128)(2,1)}, u32[]{:S(2)}) copy-start(bf16[1,2048,32]{1,2,0:T(8,128)(2,1)} %param.11) | copy-start | bytes 393220
  434.4 6.4 %copy-start.7 = (bf16[2048,32]{0,1:T(8,128)(2,1)S(1)}, bf16[2048,32]{0,1:T(8,128)(2,1)}, u32[]{:S(2)}) copy-start(bf16[2048,32]{0,1:T(8,128)(2,1)} %copy-done.6) | copy-start | bytes 393220
  434.4 46.8 %all-to-all-start.3 = ((bf16[16,56,1024]{2,1,0:T(8,128)(2,1)}), bf16[16,56,1024]{2,1,0:T(8,128)(2,1)S(1)}, u32[]{:S(2)}, u32[]{:S(2)}) async-start(bf16[16,56,1024]{2,1,0:T(8,128)(2,1)} %copy.79), calls=%async_computation.5 | async-start | bytes 3670016 | tf_op jit(solution)/shard_map/all_to_all | solution.py:72
  486.1 5.9 %copy-start.1 = (bf16[64,2048]{1,0:T(8,128)(2,1)S(1)}, bf16[64,2048]{1,0:T(8,128)(2,1)}, u32[]{:S(2)}) copy-start(bf16[64,2048]{1,0:T(8,128)(2,1)} %copy-done) | copy-start | bytes 786436
  533.6 1.4 collective-permute-start.6
Sparse Core Ops, SparseCore 0:
  94.9 68.7 reduce-scatter.2
  166.9 24.9 all-gather.2
  331.1 66.1 reduce-scatter.4
  400.5 24.9 all-gather.4
where the time goes:
time: 550 us; the launch traced here: 543 us
  waiting for transfers between devices  271 us (49%)
  blocking collectives  141 us (26%)
  matrix products  37.7 us (7%)
  local copies, waits for them, and re-layouts  32.7 us (6%)
  other arithmetic  29.4 us (5%)
  starting transfers between devices  16.7 us (3%)
  between operations  14.4 us (3%)
    reduce_scatter x2, waiting for transfers between devices, expert_layer(): summed = lax.psum_scatter(both, 'fsdp', scatter_dimension=0, tiled=True)  133 us
    all_to_all x2, blocking collectives, expert_layer(): arrived = lax.all_to_all(outgoing, ('fsdp', 'expert'), 0, 0, tiled=True)  101 us
    all_to_all x2, waiting for transfers between devices, expert_layer(): lax.all_to_all(produced.reshape(peers, local_experts * capacity, chunk),...  79.2 us
    all_gather x2, waiting for transfers between devices, expert_layer(): inner_all = lax.all_gather(inner_act, 'fsdp', axis=0, tiled=True)  50.3 us
    psum x1, blocking collectives, body(): totals = lax.psum(jnp.stack(squares), ('section', 'fsdp', 'expert'))  39.4 us
    all_to_all x2, starting transfers between devices, expert_layer(): lax.all_to_all(produced.reshape(peers, local_experts * capacity, chunk),...  11.7 us
    dot_general x2, matrix products, expert_layer(): jnp.einsum('sjch,jhd->sjcd', inner_all, down_w, preferred_element_type=jn...  11.6 us
  transfers between devices with their start and end apart: 13, of which 8 were waited for; matrix products, arithmetic and copies ran while one was open for 5% of the time, Pallas kernels for 0%

commit v1 on v0

--- a/solution.py
+++ b/solution.py
@@ -6,6 +6,28 @@
 TOP = 6
 BLOCK = 64
 epsilon = 1e-06
+
+
+def split_up(value, dim, size):
+    before, after = (value.shape[:dim], value.shape[dim + 1 :])
+    return jnp.moveaxis(value.reshape(*before, size, -1, *after), dim, 0)
+
+
+def joined_along(blocks, dim):
+    blocks = jnp.moveaxis(blocks, 0, dim)
+    dims = blocks.shape
+    return blocks.reshape(*dims[:dim], dims[dim] * dims[dim + 1], *dims[dim + 2 :])
+
+
+def rotated_exchange(array, axis, split_dim, concat_dim):
+    count, index = (lax.axis_size(axis), lax.axis_index(axis))
+    blocks = split_up(array, split_dim, count)
+    outs = [blocks[index]]
+    for step in range(1, count):
+        sent = blocks[(index + step) % count]
+        outs.append(lax.ppermute(sent, axis, [(i, (i + step) % count) for i in range(count)]))
+    blocks = jnp.stack(outs)[(index - jnp.arange(count)) % count]
+    return joined_along(blocks, concat_dim)
 
 
 def other_section(value):
@@ -69,12 +91,8 @@
     produced = jnp.einsum(
         "sjch,jhd->sjcd", inner_all, down_w, preferred_element_type=jnp.float32
     ).astype(jnp.bfloat16)
-    returned = lax.all_to_all(
-        produced.reshape(peers, local_experts * capacity, chunk),
-        ("fsdp", "expert"),
-        0,
-        0,
-        tiled=True,
+    returned = rotated_exchange(
+        produced.reshape(peers, local_experts * capacity, chunk), ("fsdp", "expert"), 0, 0
     )
     flat_out = (
         returned.reshape(fsdp_count, expert_devices, local_experts * capacity, chunk)

time: 550 us -> 567 us (1.031)
  waiting for transfers between devices: 271 us -> 213 us
  starting transfers between devices: 16.7 us -> 67.4 us
  local copies, waits for them, and re-layouts: 32.7 us -> 47.5 us
  blocking collectives: 141 us -> 148 us
    all_to_all x2 -> x0, waiting for transfers between devices: 79.2 us -> none  [expert_layer(): lax.all_to_all(produced.reshape(peers, local_experts * capacity, chunk),...]
    ppermute x0 -> x30, starting transfers between devices: none -> 63.2 us  [rotated_exchange(): lax.ppermute(sent, axis, [(i, (i + step) % count) for i in range(count)])]
    ppermute x0 -> x30, waiting for transfers between devices: none -> 25.4 us  [rotated_exchange(): lax.ppermute(sent, axis, [(i, (i + step) % count) for i in range(count)])]
    all_to_all x2 -> x0, starting transfers between devices: 11.7 us -> none  [expert_layer(): lax.all_to_all(produced.reshape(peers, local_experts * capacity, chunk),...]
    dynamic_slice x0 -> x2, local copies, waits for them, and re-layouts: none -> 10.8 us  [rotated_exchange(): sent = blocks[(index + step) % count]]
    reshape x4 -> x0, local copies, waits for them, and re-layouts: 8.3 us -> none  [the longest x2 4.52 us: expert_layer(): produced.reshape(peers, local_experts * capacity, chunk)]
  transfers between devices with their start and end apart: 13 -> 41, of which waited for: 8 -> 18; matrix products, arithmetic and copies ran while one was open for 5% -> 5% of each run, Pallas kernels for 0% -> 0%
where the time goes in v1:
time: 567 us; the launch traced here: 558 us
  waiting for transfers between devices  213 us (38%)
  blocking collectives  148 us (26%)
  starting transfers between devices  67.4 us (12%)
  local copies, waits for them, and re-layouts  47.5 us (8%)
  matrix products  37.7 us (7%)
  other arithmetic  29.7 us (5%)
  between operations  15.2 us (3%)
    reduce_scatter x2, waiting for transfers between devices, expert_layer(): summed = lax.psum_scatter(both, 'fsdp', scatter_dimension=0, tiled=True)  131 us
    all_to_all x2, blocking collectives, expert_layer(): arrived = lax.all_to_all(outgoing, ('fsdp', 'expert'), 0, 0, tiled=True)  106 us
    ppermute x30, starting transfers between devices, rotated_exchange(): lax.ppermute(sent, axis, [(i, (i + step) % count) for i in range(count)])  63.2 us
    all_gather x2, waiting for transfers between devices, expert_layer(): inner_all = lax.all_gather(inner_act, 'fsdp', axis=0, tiled=True)  47.4 us
    psum x1, blocking collectives, body(): totals = lax.psum(jnp.stack(squares), ('section', 'fsdp', 'expert'))  42.1 us
    ppermute x30, waiting for transfers between devices, rotated_exchange(): lax.ppermute(sent, axis, [(i, (i + step) % count) for i in range(count)])  25.4 us
    dot_general x2, matrix products, expert_layer(): jnp.einsum('sjch,jhd->sjcd', inner_all, down_w, preferred_element_type=jn...  11.6 us
  transfers between devices with their start and end apart: 41, of which 18 were waited for; matrix products, arithmetic and copies ran while one was open for 5% of the time, Pallas kernels for 0%

profile of v1, /device:TPU:0, one launch (start us, length us, event | category | flops | bytes accessed | tf_op | source)
XLA Modules:
  0.0 558.1 jit_solution(2701070334988508167)
XLA Ops:
  10.1 7.8 %collective-permute-done = s32[128,6]{0,1:T(8,128)S(1)} collective-permute-done((s32[128,6]{0,1:T(8,128)S(1)}, s32[128,6]{0,1:T(8,128)S(1)}, u32[]{:S(2)}, u32[]{:S(2)}) %collective-permute-start) | collective-permute-done | bytes 3104 | tf_op jit(solution)/shard_map/ppermute | solution.py:34
  21.5 2.9 convolution_convert_fusion.1
  24.4 4.6 reshape.193
  29.5 52.1 %all_to_all.10 = bf16[16,56,1024]{2,1,0:T(8,128)(2,1)S(1)} all-to-all(bf16[16,56,1024]{2,1,0:T(8,128)(2,1)S(1)} %bitcast.386), channel_id=1, replica_groups=mesh['section'=2,'fsdp'=2,'expert'=8] {'fsdp','expert'}, dimensions={0} | all-to-all | bytes 3670016 | tf_op jit(solution)/shard_map/all_to_all | solution.py:81
  82.6 4.6 fusion.27
  87.2 4.6 fusion.30
  91.8 3.1 pad_maximum_fusion
  94.9 2.0 collective-permute-start.3
  98.9 64.9 %reduce-scatter.3.cloned.1.call-done = f32[8,4,14,1536]{3,0,2,1:T(8,128)} async-done(((f32[16,4,14,1536]{3,0,2,1:T(8,128)}), f32[8,4,14,1536]{3,0,2,1:T(8,128)}) %reduce-scatter.3.cloned.1.call-update) | async-done | bytes 2752528 | tf_op jit(solution)/shard_map/reduce_scatter | solution.py:86
  163.8 3.0 fusion.43
  168.9 23.1 %all-gather.3.cloned.1.call-done = bf16[16,4,14,768]{3,0,2,1:T(8,128)(2,1)} async-done(((bf16[8,4,14,768]{3,0,2,1:T(8,128)(2,1)}), bf16[16,4,14,768]{3,0,2,1:T(8,128)(2,1)}) %all-gather.3.cloned.1.call-update) | async-done | bytes 1376272 | tf_op jit(solution)/shard_map/all_gather | solution.py:90
  192.0 4.9 fusion.24
  196.9 5.4 constant_dynamic-slice_fusion.19
  202.4 1.5 collective-permute-start.6
  204.0 1.5 collective-permute-start.7
  205.5 2.4 collective-permute-start.8
  208.0 1.5 collective-permute-start.9
  209.5 2.5 collective-permute-start.10
  212.8 2.1 collective-permute-start.11
  214.9 1.5 collective-permute-start.12
  216.4 7.8 %collective-permute-done.8 = bf16[1,56,1024]{2,1,0:T(8,128)(2,1)S(1)} collective-permute-done((bf16[1,56,1024]{2,1,0:T(8,128)(2,1)S(1)}, bf16[1,56,1024]{2,1,0:T(8,128)(2,1)S(1)}, u32[]{:S(2)}, u32[]{:S(2)}) %collective-permute-start.8) | collective-permute-done | bytes 114720 | tf_op jit(solution)/shard_map/ppermute | solution.py:28
  224.7 1.7 collective-permute-done.9
  228.4 3.1 collective-permute-start.16
  231.5 8.4 %collective-permute-start.17 = (bf16[1,56,1024]{2,1,0:T(8,128)(2,1)S(1)}, bf16[1,56,1024]{2,1,0:T(8,128)(2,1)S(1)}, u32[]{:S(2)}, u32[]{:S(2)}) collective-permute-start(bf16[1,56,1024]{2,1,0:T(8,128)(2,1)S(1)} %bitcast.406), channel_id=1, source_target_pairs={{0,12},{1,13},{2,14},{3,15},{4,0},{5,1},{6,2},{7,3},{8,4},{9,5},{1... | collective-permute-start | bytes 344072 | tf_op jit(solution)/shard_map/ppermute | solution.py:28
  240.0 4.7 collective-permute-start.19
  245.1 1.8 collective-permute-done.18
  246.9 1.8 collective-permute-done.19
  251.0 2.2 gather_fusion
  253.2 1.9 copy.208
  255.6 2.5 gather_fusion.2
  258.1 1.6 reshape.247
  259.7 4.3 multiply_reduce_fusion.1
  265.5 2.3 reshape.198
  267.7 2.0 copy.216
  269.8 53.9 %all_to_all.11 = bf16[16,56,1024]{2,1,0:T(8,128)(2,1)S(1)} all-to-all(bf16[16,56,1024]{2,1,0:T(8,128)(2,1)S(1)} %bitcast.388), channel_id=1, replica_groups=mesh['section'=2,'fsdp'=2,'expert'=8] {'fsdp','expert'}, dimensions={0} | all-to-all | bytes 3670016 | tf_op jit(solution)/shard_map/all_to_all | solution.py:81
  324.7 6.4 %fusion.36 = f32[16,4,14,768]{3,0,2,1:T(8,128)S(1)} fusion(bf16[16,4,14,1024]{3,0,2,1:T(8,128)(2,1)S(1)} %bitcast.398, bf16[4,1024,768]{2,1,0:T(8,128)(2,1)} %collective-permute-done.4, pred[]{:T(512)S(6)} %eq.158, bf16[1,4,1024,768]{3,2,1,0:T(8,128)(2,1)} %param.12), kind=kOutput, calls=%fused_computation.38 | convolution fusion | flops 1412431872 | bytes 17170432 | tf_op jit(solution)/shard_map/sjcd,jdh->sjch/dot_general | solution.py:83
  331.1 6.4 %fusion.39 = f32[16,4,14,768]{3,0,2,1:T(8,128)S(1)} fusion(bf16[16,4,14,1024]{3,0,2,1:T(8,128)(2,1)S(1)} %bitcast.399, bf16[4,1024,768]{2,1,0:T(8,128)(2,1)} %collective-permute-done.5, pred[]{:T(512)S(6)} %eq.158, bf16[1,4,1024,768]{3,2,1,0:T(8,128)(2,1)} %param.13), kind=kOutput, calls=%fused_computation.39 | convolution fusion | flops 1412431872 | bytes 17170432 | tf_op jit(solution)/shard_map/sjcd,jdh->sjch/dot_general | solution.py:84
  337.5 3.1 pad_maximum_fusion.1
  340.7 66.3 %reduce-scatter.5.cloned.1.call-done = f32[8,4,14,1536]{3,0,2,1:T(8,128)} async-done(((f32[16,4,14,1536]{3,0,2,1:T(8,128)}), f32[8,4,14,1536]{3,0,2,1:T(8,128)}) %reduce-scatter.5.cloned.1.call-update) | async-done | bytes 2752528 | tf_op jit(solution)/shard_map/reduce_scatter | solution.py:86
  407.0 3.0 fusion.42
  410.9 24.3 %all-gather.5.cloned.1.call-done = bf16[16,4,14,768]{3,0,2,1:T(8,128)(2,1)} async-done(((bf16[8,4,14,768]{3,0,2,1:T(8,128)(2,1)}), bf16[16,4,14,768]{3,0,2,1:T(8,128)(2,1)}) %all-gather.5.cloned.1.call-update) | async-done | bytes 1376272 | tf_op jit(solution)/shard_map/all_gather | solution.py:90
  435.2 6.7 %fusion.33 = bf16[4,1024,16,14]{1,2,3,0:T(8,128)(2,1)S(1)} fusion(bf16[16,4,14,768]{3,0,2,1:T(8,128)(2,1)} %all-gather.5.cloned.1.call-done, bf16[4,768,1024]{2,1,0:T(8,128)(2,1)} %collective-permute-done.3, pred[]{:T(512)S(6)} %eq.158, bf16[1,4,768,1024]{3,2,1,0:T(8,128)(2,1)} %param.14), kind=kOutput, calls=%fused_computation.37 | convolution fusion | flops 1413349376 | bytes 15794177 | tf_op jit(solution)/shard_map/sjch,jhd->sjcd/dot_general | solution.py:91
  441.9 5.4 constant_dynamic-slice_fusion.2
  447.3 1.5 collective-permute-start.21
  448.9 1.5 collective-permute-start.22
  450.5 2.4 collective-permute-start.23
  453.0 1.5 collective-permute-start.24
  454.5 2.5 collective-permute-start.25
  457.8 2.1 collective-permute-start.26
  459.9 1.5 collective-permute-start.27
  461.4 4.5 collective-permute-done.23
  467.2 4.6 collective-permute-start.30
  471.8 4.6 collective-permute-start.31
  476.4 4.1 collective-permute-start.32
  480.6 2.5 collective-permute-start.33
  484.8 3.0 collective-permute-done.33
  487.7 1.5 collective-permute-done.34
  491.7 2.2 gather_fusion.1
  493.8 1.9 copy.249
  496.3 2.5 gather_fusion.3
  498.7 1.6 reshape.251
  500.3 4.3 multiply_reduce_fusion
  505.4 1.4 pad_maximum_fusion.2
  506.7 42.1 %psum.7 = f32[2]{0:T(128)S(1)} all-reduce(f32[2]{0:T(128)S(1)} %pad_maximum_fusion.2), channel_id=1, replica_groups=mesh['section'=2,'fsdp'=2,'expert'=8] {'section','fsdp','expert'}, use_global_device_ids=true, to_apply=%region_20.22 | all-reduce | flops 2 | bytes 16 | tf_op jit(solution)/shard_map/psum | solution.py:131
  (197 shorter events, 31.8 us)
Async XLA Ops:
  7.2 156.6 %reduce-scatter.3.cloned.1.call-start = ((), (), s32[]{:S(2)}) async-start(), calls=%async_computation.4 | async-start | bytes 8257536 | tf_op jit(solution)/shard_map/reduce_scatter | solution.py:86
  7.2 75.4 %collective-permute-start.4 = (bf16[4,1024,768]{2,1,0:T(8,128)(2,1)}, bf16[4,1024,768]{2,1,0:T(8,128)(2,1)}, u32[]{:S(2)}, u32[]{:S(2)}) collective-permute-start(bf16[4,1024,768]{2,1,0:T(8,128)(2,1)} %bitcast.435), channel_id=1, source_target_pairs={{0,16},{16,0},{1,17},{17,1},{2,18},{18,2},{3,19},{19,3},{4,20},{20... | collective-permute-start | bytes 18874376 | tf_op jit(solution)/shard_map/ppermute | solution.py:34
  8.5 9.4 %collective-permute-start = (s32[128,6]{0,1:T(8,128)S(1)}, s32[128,6]{0,1:T(8,128)S(1)}, u32[]{:S(2)}, u32[]{:S(2)}) collective-permute-start(s32[128,6]{0,1:T(8,128)S(1)} %bitcast.434), channel_id=1, source_target_pairs={{0,16},{16,0},{1,17},{17,1},{2,18},{18,2},{3,19},{19,3},{4,20},{20... | collective-permute-start | bytes 9224 | tf_op jit(solution)/shard_map/ppermute | solution.py:34
  8.5 12.3 %collective-permute-start.1 = (f32[2048]{0:T(1024)}, f32[2048]{0:T(1024)S(1)}, u32[]{:S(2)}, u32[]{:S(2)}) collective-permute-start(f32[2048]{0:T(1024)} %bitcast.432), channel_id=1, source_target_pairs={{0,16},{16,0},{1,17},{17,1},{2,18},{18,2},{3,19},{19,3},{4,20},{20... | collective-permute-start | bytes 24584 | tf_op jit(solution)/shard_map/ppermute | solution.py:34
  9.0 78.2 %collective-permute-start.5 = (bf16[4,1024,768]{2,1,0:T(8,128)(2,1)}, bf16[4,1024,768]{2,1,0:T(8,128)(2,1)}, u32[]{:S(2)}, u32[]{:S(2)}) collective-permute-start(bf16[4,1024,768]{2,1,0:T(8,128)(2,1)} %bitcast.436), channel_id=1, source_target_pairs={{0,16},{16,0},{1,17},{17,1},{2,18},{18,2},{3,19},{19,3},{4,20},{20... | collective-permute-start | bytes 18874376 | tf_op jit(solution)/shard_map/ppermute | solution.py:34
  94.9 2.1 copy-start.6
  94.9 97.1 %all-gather.3.cloned.1.call-start = ((), (), s32[]{:S(2)}) async-start(), calls=%async_computation.5 | async-start | bytes 2064384 | tf_op jit(solution)/shard_map/all_gather | solution.py:90
  94.9 74.0 %collective-permute-start.3 = (bf16[4,768,1024]{2,1,0:T(8,128)(2,1)}, bf16[4,768,1024]{2,1,0:T(8,128)(2,1)}, u32[]{:S(2)}, u32[]{:S(2)}) collective-permute-start(bf16[4,768,1024]{2,1,0:T(8,128)(2,1)} %bitcast.437), channel_id=1, source_target_pairs={{0,16},{16,0},{1,17},{17,1},{2,18},{18,2},{3,19},{19,3},{4,20},{20... | collective-permute-start | bytes 18874376 | tf_op jit(solution)/shard_map/ppermute | solution.py:34
  96.9 71.5 %collective-permute-start.2 = (bf16[2048,32]{0,1:T(8,128)(2,1)S(1)}, bf16[2048,32]{0,1:T(8,128)(2,1)S(1)}, u32[]{:S(2)}, u32[]{:S(2)}) collective-permute-start(bf16[2048,32]{0,1:T(8,128)(2,1)S(1)} %bitcast.438), channel_id=1, source_target_pairs={{0,16},{16,0},{1,17},{17,1},{2,18},{18,2},{3,19},{19,3},{4,20},{20... | collective-permute-start | bytes 393224 | tf_op jit(solution)/shard_map/ppermute | solution.py:34
  98.9 69.5 %copy-start.4 = (bf16[128,2048]{1,0:T(8,128)(2,1)S(1)}, bf16[128,2048]{1,0:T(8,128)(2,1)}, u32[]{:S(2)}) copy-start(bf16[128,2048]{1,0:T(8,128)(2,1)} %param.9) | copy-start | bytes 1572868
  166.8 240.1 %reduce-scatter.5.cloned.1.call-start = ((), (), s32[]{:S(2)}) async-start(), calls=%async_computation.6 | async-start | bytes 8257536 | tf_op jit(solution)/shard_map/reduce_scatter | solution.py:86
  168.4 28.5 %copy-start.8 = (bf16[2048,32]{0,1:T(8,128)(2,1)}, bf16[2048,32]{0,1:T(8,128)(2,1)S(1)}, u32[]{:S(2)}) copy-start(bf16[2048,32]{0,1:T(8,128)(2,1)S(1)} %collective-permute-done.2) | copy-start | bytes 393220
  202.4 10.4 %collective-permute-start.6 = (bf16[1,56,1024]{2,1,0:T(8,128)(2,1)S(1)}, bf16[1,56,1024]{2,1,0:T(8,128)(2,1)S(1)}, u32[]{:S(2)}, u32[]{:S(2)}) collective-permute-start(bf16[1,56,1024]{2,1,0:T(8,128)(2,1)S(1)} %bitcast.428), channel_id=1, source_target_pairs={{0,1},{1,2},{2,3},{3,4},{4,5},{5,6},{6,7},{7,8},{8,9},{9,10},{10,1... | collective-permute-start | bytes 344072 | tf_op jit(solution)/shard_map/ppermute | solution.py:28
  204.0 10.9 %collective-permute-start.7 = (bf16[1,56,1024]{2,1,0:T(8,128)(2,1)S(1)}, bf16[1,56,1024]{2,1,0:T(8,128)(2,1)S(1)}, u32[]{:S(2)}, u32[]{:S(2)}) collective-permute-start(bf16[1,56,1024]{2,1,0:T(8,128)(2,1)S(1)} %bitcast.426), channel_id=1, source_target_pairs={{0,2},{1,3},{2,4},{3,5},{4,6},{5,7},{6,8},{7,9},{8,10},{9,11},{10,... | collective-permute-start | bytes 344072 | tf_op jit(solution)/shard_map/ppermute | solution.py:28
  205.5 18.7 %collective-permute-start.8 = (bf16[1,56,1024]{2,1,0:T(8,128)(2,1)S(1)}, bf16[1,56,1024]{2,1,0:T(8,128)(2,1)S(1)}, u32[]{:S(2)}, u32[]{:S(2)}) collective-permute-start(bf16[1,56,1024]{2,1,0:T(8,128)(2,1)S(1)} %bitcast.424), channel_id=1, source_target_pairs={{0,3},{1,4},{2,5},{3,6},{4,7},{5,8},{6,9},{7,10},{8,11},{9,12},{10... | collective-permute-start | bytes 344072 | tf_op jit(solution)/shard_map/ppermute | solution.py:28
  208.0 18.4 %collective-permute-start.9 = (bf16[1,56,1024]{2,1,0:T(8,128)(2,1)S(1)}, bf16[1,56,1024]{2,1,0:T(8,128)(2,1)S(1)}, u32[]{:S(2)}, u32[]{:S(2)}) collective-permute-start(bf16[1,56,1024]{2,1,0:T(8,128)(2,1)S(1)} %bitcast.422), channel_id=1, source_target_pairs={{0,4},{1,5},{2,6},{3,7},{4,8},{5,9},{6,10},{7,11},{8,12},{9,13},{1... | collective-permute-start | bytes 344072 | tf_op jit(solution)/shard_map/ppermute | solution.py:28
  209.5 17.5 %collective-permute-start.10 = (bf16[1,56,1024]{2,1,0:T(8,128)(2,1)S(1)}, bf16[1,56,1024]{2,1,0:T(8,128)(2,1)S(1)}, u32[]{:S(2)}, u32[]{:S(2)}) collective-permute-start(bf16[1,56,1024]{2,1,0:T(8,128)(2,1)S(1)} %bitcast.420), channel_id=1, source_target_pairs={{0,5},{1,6},{2,7},{3,8},{4,9},{5,10},{6,11},{7,12},{8,13},{9,14},{... | collective-permute-start | bytes 344072 | tf_op jit(solution)/shard_map/ppermute | solution.py:28
  212.8 15.6 %collective-permute-start.11 = (bf16[1,56,1024]{2,1,0:T(8,128)(2,1)S(1)}, bf16[1,56,1024]{2,1,0:T(8,128)(2,1)S(1)}, u32[]{:S(2)}, u32[]{:S(2)}) collective-permute-start(bf16[1,56,1024]{2,1,0:T(8,128)(2,1)S(1)} %bitcast.418), channel_id=1, source_target_pairs={{0,6},{1,7},{2,8},{3,9},{4,10},{5,11},{6,12},{7,13},{8,14},{9,15},... | collective-permute-start | bytes 344072 | tf_op jit(solution)/shard_map/ppermute | solution.py:28
  214.9 16.6 %collective-permute-start.12 = (bf16[1,56,1024]{2,1,0:T(8,128)(2,1)S(1)}, bf16[1,56,1024]{2,1,0:T(8,128)(2,1)S(1)}, u32[]{:S(2)}, u32[]{:S(2)}) collective-permute-start(bf16[1,56,1024]{2,1,0:T(8,128)(2,1)S(1)} %bitcast.416), channel_id=1, source_target_pairs={{0,7},{1,8},{2,9},{3,10},{4,11},{5,12},{6,13},{7,14},{8,15},{9,0},... | collective-permute-start | bytes 344072 | tf_op jit(solution)/shard_map/ppermute | solution.py:28
  224.3 15.6 %collective-permute-start.13 = (bf16[1,56,1024]{2,1,0:T(8,128)(2,1)S(1)}, bf16[1,56,1024]{2,1,0:T(8,128)(2,1)S(1)}, u32[]{:S(2)}, u32[]{:S(2)}) collective-permute-start(bf16[1,56,1024]{2,1,0:T(8,128)(2,1)S(1)} %bitcast.414), channel_id=1, source_target_pairs={{0,8},{1,9},{2,10},{3,11},{4,12},{5,13},{6,14},{7,15},{8,0},{9,1},... | collective-permute-start | bytes 344072 | tf_op jit(solution)/shard_map/ppermute | solution.py:28
  226.4 13.5 %collective-permute-start.14 = (bf16[1,56,1024]{2,1,0:T(8,128)(2,1)S(1)}, bf16[1,56,1024]{2,1,0:T(8,128)(2,1)S(1)}, u32[]{:S(2)}, u32[]{:S(2)}) collective-permute-start(bf16[1,56,1024]{2,1,0:T(8,128)(2,1)S(1)} %bitcast.412), channel_id=1, source_target_pairs={{0,9},{1,10},{2,11},{3,12},{4,13},{5,14},{6,15},{7,0},{8,1},{9,2},... | collective-permute-start | bytes 344072 | tf_op jit(solution)/shard_map/ppermute | solution.py:28
  227.1 17.6 %collective-permute-start.15 = (bf16[1,56,1024]{2,1,0:T(8,128)(2,1)S(1)}, bf16[1,56,1024]{2,1,0:T(8,128)(2,1)S(1)}, u32[]{:S(2)}, u32[]{:S(2)}) collective-permute-start(bf16[1,56,1024]{2,1,0:T(8,128)(2,1)S(1)} %bitcast.410), channel_id=1, source_target_pairs={{0,10},{1,11},{2,12},{3,13},{4,14},{5,15},{6,0},{7,1},{8,2},{9,3},... | collective-permute-start | bytes 344072 | tf_op jit(solution)/shard_map/ppermute | solution.py:28
  228.4 16.6 %collective-permute-start.16 = (bf16[1,56,1024]{2,1,0:T(8,128)(2,1)S(1)}, bf16[1,56,1024]{2,1,0:T(8,128)(2,1)S(1)}, u32[]{:S(2)}, u32[]{:S(2)}) collective-permute-start(bf16[1,56,1024]{2,1,0:T(8,128)(2,1)S(1)} %bitcast.408), channel_id=1, source_target_pairs={{0,11},{1,12},{2,13},{3,14},{4,15},{5,0},{6,1},{7,2},{8,3},{9,4},{... | collective-permute-start | bytes 344072 | tf_op jit(solution)/shard_map/ppermute | solution.py:28
  231.5 13.5 %collective-permute-start.17 = (bf16[1,56,1024]{2,1,0:T(8,128)(2,1)S(1)}, bf16[1,56,1024]{2,1,0:T(8,128)(2,1)S(1)}, u32[]{:S(2)}, u32[]{:S(2)}) collective-permute-start(bf16[1,56,1024]{2,1,0:T(8,128)(2,1)S(1)} %bitcast.406), channel_id=1, source_target_pairs={{0,12},{1,13},{2,14},{3,15},{4,0},{5,1},{6,2},{7,3},{8,4},{9,5},{1... | collective-permute-start | bytes 344072 | tf_op jit(solution)/shard_map/ppermute | solution.py:28
  239.9 7.0 %collective-permute-start.18 = (bf16[1,56,1024]{2,1,0:T(8,128)(2,1)S(1)}, bf16[1,56,1024]{2,1,0:T(8,128)(2,1)S(1)}, u32[]{:S(2)}, u32[]{:S(2)}) collective-permute-start(bf16[1,56,1024]{2,1,0:T(8,128)(2,1)S(1)} %bitcast.404), channel_id=1, source_target_pairs={{0,13},{1,14},{2,15},{3,0},{4,1},{5,2},{6,3},{7,4},{8,5},{9,6},{10... | collective-permute-start | bytes 344072 | tf_op jit(solution)/shard_map/ppermute | solution.py:28
  240.0 8.7 %collective-permute-start.19 = (bf16[1,56,1024]{2,1,0:T(8,128)(2,1)S(1)}, bf16[1,56,1024]{2,1,0:T(8,128)(2,1)S(1)}, u32[]{:S(2)}, u32[]{:S(2)}) collective-permute-start(bf16[1,56,1024]{2,1,0:T(8,128)(2,1)S(1)} %bitcast.402), channel_id=1, source_target_pairs={{0,14},{1,15},{2,0},{3,1},{4,2},{5,3},{6,4},{7,5},{8,6},{9,7},{10,... | collective-permute-start | bytes 344072 | tf_op jit(solution)/shard_map/ppermute | solution.py:28
  244.7 5.1 collective-permute-start.20
  249.8 1.2 copy-start.2
  259.7 4.3 copy-start.5
  264.7 145.6 %copy-start = (bf16[64,2048]{1,0:T(8,128)(2,1)}, bf16[64,2048]{1,0:T(8,128)(2,1)S(1)}, u32[]{:S(2)}) copy-start(bf16[64,2048]{1,0:T(8,128)(2,1)S(1)} %get-tuple-element.13) | copy-start | bytes 786436
  340.6 69.8 %copy-start.7 = (bf16[1,2048,32]{1,2,0:T(8,128)(2,1)S(1)}, bf16[1,2048,32]{1,2,0:T(8,128)(2,1)}, u32[]{:S(2)}) copy-start(bf16[1,2048,32]{1,2,0:T(8,128)(2,1)} %param.11) | copy-start | bytes 393220
  340.7 69.8 %copy-start.9 = (bf16[2048,32]{0,1:T(8,128)(2,1)S(1)}, bf16[2048,32]{0,1:T(8,128)(2,1)}, u32[]{:S(2)}) copy-start(bf16[2048,32]{0,1:T(8,128)(2,1)} %copy-done.8) | copy-start | bytes 393220
  340.7 94.5 %all-gather.5.cloned.1.call-start = ((), (), s32[]{:S(2)}) async-start(), calls=%async_computation.7 | async-start | bytes 2064384 | tf_op jit(solution)/shard_map/all_gather | solution.py:90
  447.3 10.4 %collective-permute-start.21 = (bf16[1,56,1024]{2,1,0:T(8,128)(2,1)S(1)}, bf16[1,56,1024]{2,1,0:T(8,128)(2,1)S(1)}, u32[]{:S(2)}, u32[]{:S(2)}) collective-permute-start(bf16[1,56,1024]{2,1,0:T(8,128)(2,1)S(1)} %bitcast.429), channel_id=1, source_target_pairs={{0,1},{1,2},{2,3},{3,4},{4,5},{5,6},{6,7},{7,8},{8,9},{9,10},{10,1... | collective-permute-start | bytes 344072 | tf_op jit(solution)/shard_map/ppermute | solution.py:28
  448.9 10.9 %collective-permute-start.22 = (bf16[1,56,1024]{2,1,0:T(8,128)(2,1)S(1)}, bf16[1,56,1024]{2,1,0:T(8,128)(2,1)S(1)}, u32[]{:S(2)}, u32[]{:S(2)}) collective-permute-start(bf16[1,56,1024]{2,1,0:T(8,128)(2,1)S(1)} %bitcast.427), channel_id=1, source_target_pairs={{0,2},{1,3},{2,4},{3,5},{4,6},{5,7},{6,8},{7,9},{8,10},{9,11},{10,... | collective-permute-start | bytes 344072 | tf_op jit(solution)/shard_map/ppermute | solution.py:28
  450.5 15.4 %collective-permute-start.23 = (bf16[1,56,1024]{2,1,0:T(8,128)(2,1)S(1)}, bf16[1,56,1024]{2,1,0:T(8,128)(2,1)S(1)}, u32[]{:S(2)}, u32[]{:S(2)}) collective-permute-start(bf16[1,56,1024]{2,1,0:T(8,128)(2,1)S(1)} %bitcast.425), channel_id=1, source_target_pairs={{0,3},{1,4},{2,5},{3,6},{4,7},{5,8},{6,9},{7,10},{8,11},{9,12},{10... | collective-permute-start | bytes 344072 | tf_op jit(solution)/shard_map/ppermute | solution.py:28
  453.0 13.6 %collective-permute-start.24 = (bf16[1,56,1024]{2,1,0:T(8,128)(2,1)S(1)}, bf16[1,56,1024]{2,1,0:T(8,128)(2,1)S(1)}, u32[]{:S(2)}, u32[]{:S(2)}) collective-permute-start(bf16[1,56,1024]{2,1,0:T(8,128)(2,1)S(1)} %bitcast.423), channel_id=1, source_target_pairs={{0,4},{1,5},{2,6},{3,7},{4,8},{5,9},{6,10},{7,11},{8,12},{9,13},{1... | collective-permute-start | bytes 344072 | tf_op jit(solution)/shard_map/ppermute | solution.py:28
  454.5 12.7 %collective-permute-start.25 = (bf16[1,56,1024]{2,1,0:T(8,128)(2,1)S(1)}, bf16[1,56,1024]{2,1,0:T(8,128)(2,1)S(1)}, u32[]{:S(2)}, u32[]{:S(2)}) collective-permute-start(bf16[1,56,1024]{2,1,0:T(8,128)(2,1)S(1)} %bitcast.421), channel_id=1, source_target_pairs={{0,5},{1,6},{2,7},{3,8},{4,9},{5,10},{6,11},{7,12},{8,13},{9,14},{... | collective-permute-start | bytes 344072 | tf_op jit(solution)/shard_map/ppermute | solution.py:28
  457.8 14.0 %collective-permute-start.26 = (bf16[1,56,1024]{2,1,0:T(8,128)(2,1)S(1)}, bf16[1,56,1024]{2,1,0:T(8,128)(2,1)S(1)}, u32[]{:S(2)}, u32[]{:S(2)}) collective-permute-start(bf16[1,56,1024]{2,1,0:T(8,128)(2,1)S(1)} %bitcast.419), channel_id=1, source_target_pairs={{0,6},{1,7},{2,8},{3,9},{4,10},{5,11},{6,12},{7,13},{8,14},{9,15},... | collective-permute-start | bytes 344072 | tf_op jit(solution)/shard_map/ppermute | solution.py:28
  459.9 16.6 %collective-permute-start.27 = (bf16[1,56,1024]{2,1,0:T(8,128)(2,1)S(1)}, bf16[1,56,1024]{2,1,0:T(8,128)(2,1)S(1)}, u32[]{:S(2)}, u32[]{:S(2)}) collective-permute-start(bf16[1,56,1024]{2,1,0:T(8,128)(2,1)S(1)} %bitcast.417), channel_id=1, source_target_pairs={{0,7},{1,8},{2,9},{3,10},{4,11},{5,12},{6,13},{7,14},{8,15},{9,0},... | collective-permute-start | bytes 344072 | tf_op jit(solution)/shard_map/ppermute | solution.py:28
  465.9 14.7 %collective-permute-start.28 = (bf16[1,56,1024]{2,1,0:T(8,128)(2,1)S(1)}, bf16[1,56,1024]{2,1,0:T(8,128)(2,1)S(1)}, u32[]{:S(2)}, u32[]{:S(2)}) collective-permute-start(bf16[1,56,1024]{2,1,0:T(8,128)(2,1)S(1)} %bitcast.415), channel_id=1, source_target_pairs={{0,8},{1,9},{2,10},{3,11},{4,12},{5,13},{6,14},{7,15},{8,0},{9,1},... | collective-permute-start | bytes 344072 | tf_op jit(solution)/shard_map/ppermute | solution.py:28
  466.5 16.5 %collective-permute-start.29 = (bf16[1,56,1024]{2,1,0:T(8,128)(2,1)S(1)}, bf16[1,56,1024]{2,1,0:T(8,128)(2,1)S(1)}, u32[]{:S(2)}, u32[]{:S(2)}) collective-permute-start(bf16[1,56,1024]{2,1,0:T(8,128)(2,1)S(1)} %bitcast.413), channel_id=1, source_target_pairs={{0,9},{1,10},{2,11},{3,12},{4,13},{5,14},{6,15},{7,0},{8,1},{9,2},... | collective-permute-start | bytes 344072 | tf_op jit(solution)/shard_map/ppermute | solution.py:28
  467.2 16.9 %collective-permute-start.30 = (bf16[1,56,1024]{2,1,0:T(8,128)(2,1)S(1)}, bf16[1,56,1024]{2,1,0:T(8,128)(2,1)S(1)}, u32[]{:S(2)}, u32[]{:S(2)}) collective-permute-start(bf16[1,56,1024]{2,1,0:T(8,128)(2,1)S(1)} %bitcast.411), channel_id=1, source_target_pairs={{0,10},{1,11},{2,12},{3,13},{4,14},{5,15},{6,0},{7,1},{8,2},{9,3},... | collective-permute-start | bytes 344072 | tf_op jit(solution)/shard_map/ppermute | solution.py:28
  471.8 12.9 %collective-permute-start.31 = (bf16[1,56,1024]{2,1,0:T(8,128)(2,1)S(1)}, bf16[1,56,1024]{2,1,0:T(8,128)(2,1)S(1)}, u32[]{:S(2)}, u32[]{:S(2)}) collective-permute-start(bf16[1,56,1024]{2,1,0:T(8,128)(2,1)S(1)} %bitcast.409), channel_id=1, source_target_pairs={{0,11},{1,12},{2,13},{3,14},{4,15},{5,0},{6,1},{7,2},{8,3},{9,4},{... | collective-permute-start | bytes 344072 | tf_op jit(solution)/shard_map/ppermute | solution.py:28
  476.4 8.3 %collective-permute-start.32 = (bf16[1,56,1024]{2,1,0:T(8,128)(2,1)S(1)}, bf16[1,56,1024]{2,1,0:T(8,128)(2,1)S(1)}, u32[]{:S(2)}, u32[]{:S(2)}) collective-permute-start(bf16[1,56,1024]{2,1,0:T(8,128)(2,1)S(1)} %bitcast.407), channel_id=1, source_target_pairs={{0,12},{1,13},{2,14},{3,15},{4,0},{5,1},{6,2},{7,3},{8,4},{9,5},{1... | collective-permute-start | bytes 344072 | tf_op jit(solution)/shard_map/ppermute | solution.py:28
  480.6 7.1 %collective-permute-start.33 = (bf16[1,56,1024]{2,1,0:T(8,128)(2,1)S(1)}, bf16[1,56,1024]{2,1,0:T(8,128)(2,1)S(1)}, u32[]{:S(2)}, u32[]{:S(2)}) collective-permute-start(bf16[1,56,1024]{2,1,0:T(8,128)(2,1)S(1)} %bitcast.405), channel_id=1, source_target_pairs={{0,13},{1,14},{2,15},{3,0},{4,1},{5,2},{6,3},{7,4},{8,5},{9,6},{10... | collective-permute-start | bytes 344072 | tf_op jit(solution)/shard_map/ppermute | solution.py:28
  483.1 6.1 %collective-permute-start.34 = (bf16[1,56,1024]{2,1,0:T(8,128)(2,1)S(1)}, bf16[1,56,1024]{2,1,0:T(8,128)(2,1)S(1)}, u32[]{:S(2)}, u32[]{:S(2)}) collective-permute-start(bf16[1,56,1024]{2,1,0:T(8,128)(2,1)S(1)} %bitcast.403), channel_id=1, source_target_pairs={{0,14},{1,15},{2,0},{3,1},{4,2},{5,3},{6,4},{7,5},{8,6},{9,7},{10,... | collective-permute-start | bytes 344072 | tf_op jit(solution)/shard_map/ppermute | solution.py:28
  484.1 6.3 %collective-permute-start.35 = (bf16[1,56,1024]{2,1,0:T(8,128)(2,1)S(1)}, bf16[1,56,1024]{2,1,0:T(8,128)(2,1)S(1)}, u32[]{:S(2)}, u32[]{:S(2)}) collective-permute-start(bf16[1,56,1024]{2,1,0:T(8,128)(2,1)S(1)} %bitcast.401), channel_id=1, source_target_pairs={{0,15},{1,0},{2,1},{3,2},{4,3},{5,4},{6,5},{7,6},{8,7},{9,8},{10,9... | collective-permute-start | bytes 344072 | tf_op jit(solution)/shard_map/ppermute | solution.py:28
  490.4 1.3 copy-start.3
  500.3 4.3 copy-start.1
  548.9 1.4 collective-permute-start.36
Sparse Core Ops, SparseCore 0:
  95.0 68.7 reduce-scatter.2
  167.0 24.9 all-gather.2
  340.8 66.1 reduce-scatter.4
  410.1 24.9 all-gather.4
